TPU v7x, 256 devices: a whole 4x4x8 slice. The times are simulated.
256 devices in a mesh: gx: 4 (over z_lo), gy: 8 (over z_hi, y), gz: 8 (over x, core).
Axes of the slice: x: 4, y: 4, z: 8 (z_hi: 2, z_lo: 4; z = z_hi * 4 + z_lo), core: 2. Of those that a mesh axis runs over, the one named last changes fastest.
Arguments:
- vectors: float32 [4, 5, 125, 4, 8, 1024], P(None, None, None, 'gx', 'gy', 'gz'), may hold values from -6 to 6
- stiffness: float32 [5, 5], replicated, may hold values from -2.5 to 2.5
- flux: float32 [3, 5, 5], replicated, may hold values from -1.25 to 1.25
- penalty: float32 [3, 5], replicated, may hold values from 0.2 to 2
- local_factor: float32 [5, 5], replicated, may hold values from -2.5 to 2.5
- element_field_factor: float32 [5, 5], replicated, may hold values from -2.5 to 2.5
- aggregate: int32 [4, 8, 1024], P('gx', 'gy', 'gz'), may hold values from 0 to 1023
- coarse_inverse: float32 [20480, 5120], P(('gx', 'gy', 'gz')), may hold values from -0.078125 to 0.078125
Outputs:
- result: float32 [4, 5, 125, 4, 8, 1024], P(None, None, None, 'gx', 'gy', 'gz')
Inputs may be any that keep to these rules, and one draw needn't show every extreme that they name: aggregate numbers are counted within the elements of one index of gx.
All inputs are finite; a program needn't handle non-finite values.
Results may differ from a plain program's by a relative error of at most 0.0001.
Values sent between devices are 32-bit elements; how exact they have to be, the bound alone decides.
No kernel may reach another device: no remote copies, remote signals or barrier semaphores. Data moves between devices by JAX's collectives and lax.ppermute only.
A program may use at most 256 MiB of HBM per device.

v0:
```python
import jax
import jax.numpy as jnp
import numpy as np
from jax import lax
from jax.sharding import PartitionSpec as P

HIGH = lax.Precision.HIGHEST


def with_halo(shard, sides, width):
    for axis, dim in sides:
        size, length = (lax.axis_size(axis), shard.shape[dim])
        up = [(i, (i + 1) % size) for i in range(size - 1)]
        down = [(j, i) for i, j in up]
        last = lax.slice_in_dim(shard, length - width, length, axis=dim)
        initial = lax.slice_in_dim(shard, 0, width, axis=dim)
        before = lax.ppermute(last, axis, up)
        after = lax.ppermute(initial, axis, down)
        shard = jnp.concatenate([before, shard, after], axis=dim)
    return shard


def kron_three(first, second, third):
    return jnp.kron(jnp.kron(first, second), third)


def operator_matrix(stiffness, flux):
    unit = jnp.eye(5, dtype=jnp.float32)
    sweeps = [
        kron_three(stiffness, unit, unit),
        kron_three(unit, stiffness, unit),
        kron_three(unit, unit, stiffness),
    ]
    total = jnp.zeros((625, 625), jnp.float32)
    for axis in range(3):
        total = total + jnp.kron(flux[axis], sweeps[axis])
    return total.reshape(5, 125, 5, 125)


def face_table():
    table = np.zeros((150, 125), np.float32)
    for axis in range(3):
        for side in range(2):
            level = 4 * side
            for first in range(5):
                for second in range(5):
                    if axis == 0:
                        node = 25 * level + 5 * first + second
                    elif axis == 1:
                        node = 25 * first + 5 * level + second
                    else:
                        node = 25 * first + 5 * second + level
                    table[50 * axis + 25 * side + 5 * first + second, node] = 1.0
    return table


def operate(flat, dims, big, penalty, selects):
    vecs, fields, elements = (flat.shape[0], flat.shape[1], flat.shape[3])
    output = flat + jnp.einsum("fqgp,kgpe->kfqe", big, flat, precision=HIGH)
    faces = jnp.einsum("sq,kfqe->kfse", selects, flat, precision=HIGH)
    shaped = (vecs, fields, 25) + dims
    pairs = []
    for axis in range(3):
        minus = faces[:, :, 50 * axis : 50 * axis + 25].reshape(shaped)
        plus = faces[:, :, 50 * axis + 25 : 50 * axis + 50].reshape(shaped)
        pairs.append((minus, plus))
    neighbours = []
    stacks = [jnp.stack([pairs[axis][0], pairs[axis][1]], 0) for axis in range(3)]
    outer = [
        with_halo(stacks[0], (("gx", 4),), 1),
        with_halo(stacks[1], (("gy", 5),), 1),
        with_halo(stacks[2], (("gz", 6),), 1),
    ]
    for axis in range(3):
        count = dims[axis]
        after = lax.slice_in_dim(outer[axis][0], 2, count + 2, axis=3 + axis)
        before = lax.slice_in_dim(outer[axis][1], 0, count, axis=3 + axis)
        neighbours.append((after, before))
    terms = []
    for axis in range(3):
        minus, plus = pairs[axis]
        tau = penalty[axis][None, :, None, None, None, None]
        terms.append((tau * (minus - neighbours[axis][1])).reshape(vecs, fields, 25, elements))
        terms.append((tau * (plus - neighbours[axis][0])).reshape(vecs, fields, 25, elements))
    stacked = jnp.concatenate(terms, axis=2)
    return output + jnp.einsum("sq,kfse->kfqe", selects, stacked, precision=HIGH)


def precondition(flat, local_kron, element_field_factor, onehot, coarse_inverse):
    vecs, fields, elements = (flat.shape[0], flat.shape[1], flat.shape[3])
    fine = jnp.einsum("qp,kfpe->kfqe", local_kron, flat, precision=HIGH)
    fine = jnp.einsum("fg,kgqe->kfqe", element_field_factor, fine, precision=HIGH)
    nagg = coarse_inverse.shape[1] // fields
    means = jnp.sum(flat, axis=2) * (1.0 / 125.0)
    block = means.reshape(vecs * fields, elements)
    partial_sum = jnp.dot(block, onehot, precision=HIGH)
    restricted = lax.psum(partial_sum, ("gy", "gz"))
    merged = restricted.reshape(vecs, fields * nagg)
    owned = jnp.einsum("kc,rc->kr", merged, coarse_inverse, precision=HIGH)
    coarse = lax.all_gather(owned, ("gy", "gz"), axis=1, tiled=True)
    values = jnp.dot(coarse.reshape(vecs * fields, nagg), onehot.T, precision=HIGH)
    back = values.reshape(vecs, fields, elements)
    return fine + back[:, :, None, :]


def on_device(
    vectors, stiffness, flux, penalty, local_factor, element_field_factor, aggregate, coarse_inverse
):
    big = operator_matrix(stiffness, flux)
    local_kron = kron_three(local_factor, local_factor, local_factor)
    selects = jnp.asarray(face_table())
    dims = tuple(vectors.shape[3:])
    elements = aggregate.size
    nagg = coarse_inverse.shape[1] // vectors.shape[1]
    onehot = (
        aggregate.reshape(elements)[:, None] == jnp.arange(nagg, dtype=jnp.int32)[None, :]
    ).astype(jnp.float32)
    flat = vectors.reshape(vectors.shape[:3] + (elements,))
    for turn in range(2):
        flat = precondition(flat, local_kron, element_field_factor, onehot, coarse_inverse)
        flat = operate(flat, dims, big, penalty, selects)
    return flat.reshape(vectors.shape)


def solution(mesh):
    placed = (
        P(None, None, None, "gx", "gy", "gz"),
        P(),
        P(),
        P(),
        P(),
        P(),
        P("gx", "gy", "gz"),
        P(("gx", "gy", "gz"), None),
    )
    return jax.shard_map(
        on_device,
        mesh=mesh,
        in_specs=placed,
        out_specs=P(None, None, None, "gx", "gy", "gz"),
        check_vma=False,
    )
```

profile of v0, /device:TPU:225, one launch (start us, length us, event | category | flops | bytes accessed | tf_op | source)
XLA Modules:
  0.0 1826.5 jit_solution(4462123117621494507)
XLA Ops:
  12.3 2.8 reshape.385
  19.8 2.6 broadcast_multiply_fusion.2
  23.6 3.4 mul.353
  27.0 3.4 mul.364
  30.4 3.4 mul.374
  34.4 687.8 %all-reduce.3.cloned.1.call-done = f32[4,5120]{1,0:T(4,128)} async-done(((f32[4,5120]{1,0:T(4,128)}), f32[4,5120]{1,0:T(4,128)}) %all-reduce.3.cloned.1.call-update) | async-done | bytes 81936 | tf_op jit(solution)/shard_map/psum | solution.py:97
  724.4 117.8 %all-gather = f32[64,80,4]{1,2,0:T(4,128)S(1)} all-gather(f32[1,80,4]{1,2,0:T(4,128)S(1)} %convolution_bitcast_fusion.5), channel_id=1, replica_groups=mesh['gx'=4,'gy'=8,'gz'=8] {'gy','gz'}, dimensions={0}, use_global_device_ids=true | all-gather | bytes 83200 | tf_op jit(solution)/shard_map/all_gather | solution.py:100
  852.5 9.4 collective-permute-start.3
  876.3 4.6 fusion.9
  880.9 5.0 collective-permute-start.1
  893.5 2.8 collective-permute-done
  901.6 9.2 concatenate.27
  913.2 4.3 fusion.76
  918.6 3.8 convolution_bitcast_fusion.2
  924.2 700.6 %all-reduce.5.cloned.1.call-done = f32[4,5120]{1,0:T(4,128)} async-done(((f32[4,5120]{1,0:T(4,128)}), f32[4,5120]{1,0:T(4,128)}) %all-reduce.5.cloned.1.call-update) | async-done | bytes 81936 | tf_op jit(solution)/shard_map/psum | solution.py:97
  1627.1 118.0 %all-gather.1 = f32[64,80,4]{1,2,0:T(4,128)S(1)} all-gather(f32[1,80,4]{1,2,0:T(4,128)S(1)} %convolution_bitcast_fusion.4), channel_id=1, replica_groups=mesh['gx'=4,'gy'=8,'gz'=8] {'gy','gz'}, dimensions={0}, use_global_device_ids=true | all-gather | bytes 83200 | tf_op jit(solution)/shard_map/all_gather | solution.py:100
  1745.8 3.5 bitcast_add_fusion.2
  1755.6 9.4 collective-permute-start.9
  1776.0 6.2 fusion.12
  1782.2 5.0 collective-permute-start.7
  1793.9 5.4 collective-permute-done.6
  1804.1 3.3 concatenate.31
  1807.5 4.3 fusion.79
  1813.6 3.6 fusion
  (183 shorter events, 92.7 us)
Async XLA Ops:
  6.5 715.7 %copy-start = (f32[80,5120]{1,0:T(8,128)S(1)}, f32[80,5120]{1,0:T(8,128)}, u32[]{:S(2)}) copy-start(f32[80,5120]{1,0:T(8,128)} %param.16) | copy-start | bytes 4915204
  6.5 715.7 %all-reduce.3.cloned.1.call-start = ((), (), s32[]{:S(2)}) async-start(), calls=%async_computation | async-start | bytes 163840 | tf_op jit(solution)/shard_map/psum | solution.py:97
  10.4 1614.5 %all-reduce.5.cloned.1.call-start = ((), (), s32[]{:S(2)}) async-start(), calls=%async_computation.1 | async-start | bytes 163840 | tf_op jit(solution)/shard_map/psum | solution.py:97
  23.6 876.7 %copy-start.25 = (f32[5]{0:T(128)}, f32[5]{0:T(128)S(1)}, u32[]{:S(2)}) copy-start(f32[5]{0:T(128)S(1)} %get-tuple-element.63) | copy-start | bytes 64
  23.6 876.7 %copy-start.28 = (f32[5]{0:T(128)}, f32[5]{0:T(128)S(1)}, u32[]{:S(2)}) copy-start(f32[5]{0:T(128)S(1)} %get-tuple-element.62) | copy-start | bytes 64
  33.8 808.6 %copy-start.37 = (s32[1,1,128]{2,1,0:T(1,128)S(1)}, s32[1,1,128]{2,1,0:T(1,128)}, u32[]{:S(2)}) copy-start(s32[1,1,128]{2,1,0:T(1,128)} %param.15) | copy-start | bytes 1540
  33.9 809.0 %copy-start.24 = (f32[5,5]{1,0:T(8,128)S(1)}, f32[5,5]{1,0:T(8,128)}, u32[]{:S(2)}) copy-start(f32[5,5]{1,0:T(8,128)} %param.14) | copy-start | bytes 304
  849.4 13.8 copy-start.6
  849.4 13.8 copy-start.9
  849.4 13.8 copy-start.10
  850.6 40.6 %collective-permute-start.2 = (f32[2,4,5,25,1,1,128]{6,1,5,4,3,2,0:T(4,128)}, f32[2,4,5,25,1,1,128]{6,1,5,4,3,2,0:T(4,128)}, u32[]{:S(2)}, u32[]{:S(2)}) collective-permute-start(f32[2,4,5,25,1,1,128]{6,1,5,4,3,2,0:T(4,128)} %copy.60), channel_id=1, source_target_pairs={{0,8},{8,16},{16,24},{24,32},{32,40},{40,48},{48,56},{1,9},{9,17},... | collective-permute-start | bytes 1536008 | tf_op jit(solution)/shard_map/ppermute | solution.py:17
  852.5 39.8 %collective-permute-start.3 = (f32[2,4,5,25,1,1,128]{6,1,5,4,3,2,0:T(4,128)}, f32[2,4,5,25,1,1,128]{6,1,5,4,3,2,0:T(4,128)}, u32[]{:S(2)}, u32[]{:S(2)}) collective-permute-start(f32[2,4,5,25,1,1,128]{6,1,5,4,3,2,0:T(4,128)} %copy.60), channel_id=1, source_target_pairs={{8,0},{16,8},{24,16},{32,24},{40,32},{48,40},{56,48},{9,1},{17,9},... | collective-permute-start | bytes 1536008 | tf_op jit(solution)/shard_map/ppermute | solution.py:18
  865.2 15.7 collective-permute-start.4
  869.1 17.9 collective-permute-start.5
  874.9 21.4 %collective-permute-start = (f32[2,4,5,25,1,1,128]{6,1,5,4,3,2,0:T(4,128)}, f32[2,4,5,25,1,1,128]{6,1,5,4,3,2,0:T(4,128)}, u32[]{:S(2)}, u32[]{:S(2)}) collective-permute-start(f32[2,4,5,25,1,1,128]{6,1,5,4,3,2,0:T(4,128)} %copy.54), channel_id=1, source_target_pairs={{0,64},{64,128},{128,192},{1,65},{65,129},{129,193},{2,66},{66,130... | collective-permute-start | bytes 1536008 | tf_op jit(solution)/shard_map/ppermute | solution.py:17
  880.9 17.0 collective-permute-start.1
  1752.5 15.0 copy-start.8
  1753.7 38.0 %collective-permute-start.8 = (f32[2,4,5,25,1,1,128]{6,1,5,4,3,2,0:T(4,128)}, f32[2,4,5,25,1,1,128]{6,1,5,4,3,2,0:T(4,128)}, u32[]{:S(2)}, u32[]{:S(2)}) collective-permute-start(f32[2,4,5,25,1,1,128]{6,1,5,4,3,2,0:T(4,128)} %copy.80), channel_id=1, source_target_pairs={{0,8},{8,16},{16,24},{24,32},{32,40},{40,48},{48,56},{1,9},{9,17},... | collective-permute-start | bytes 1536008 | tf_op jit(solution)/shard_map/ppermute | solution.py:17
  1755.6 37.2 %collective-permute-start.9 = (f32[2,4,5,25,1,1,128]{6,1,5,4,3,2,0:T(4,128)}, f32[2,4,5,25,1,1,128]{6,1,5,4,3,2,0:T(4,128)}, u32[]{:S(2)}, u32[]{:S(2)}) collective-permute-start(f32[2,4,5,25,1,1,128]{6,1,5,4,3,2,0:T(4,128)} %copy.80), channel_id=1, source_target_pairs={{8,0},{16,8},{24,16},{32,24},{40,32},{48,40},{56,48},{9,1},{17,9},... | collective-permute-start | bytes 1536008 | tf_op jit(solution)/shard_map/ppermute | solution.py:18
  1766.2 33.2 %collective-permute-start.6 = (f32[2,4,5,25,1,1,128]{6,1,5,4,3,2,0:T(4,128)}, f32[2,4,5,25,1,1,128]{6,1,5,4,3,2,0:T(4,128)}, u32[]{:S(2)}, u32[]{:S(2)}) collective-permute-start(f32[2,4,5,25,1,1,128]{6,1,5,4,3,2,0:T(4,128)} %copy.75), channel_id=1, source_target_pairs={{0,64},{64,128},{128,192},{1,65},{65,129},{129,193},{2,66},{66,130... | collective-permute-start | bytes 1536008 | tf_op jit(solution)/shard_map/ppermute | solution.py:17
  1767.5 8.5 copy-start.17
  1770.2 11.9 collective-permute-start.10
  1773.6 14.8 collective-permute-start.11
  1782.2 18.7 %collective-permute-start.7 = (f32[2,4,5,25,1,1,128]{6,1,5,4,3,2,0:T(4,128)}, f32[2,4,5,25,1,1,128]{6,1,5,4,3,2,0:T(4,128)}, u32[]{:S(2)}, u32[]{:S(2)}) collective-permute-start(f32[2,4,5,25,1,1,128]{6,1,5,4,3,2,0:T(4,128)} %copy.75), channel_id=1, source_target_pairs={{64,0},{128,64},{192,128},{65,1},{129,65},{193,129},{66,2},{130,66... | collective-permute-start | bytes 1536008 | tf_op jit(solution)/shard_map/ppermute | solution.py:18
  (29 other events, 130.8 us)
Sparse Core Ops, SparseCore 0:
  10.5 711.6 all-reduce.2
  918.7 706.1 all-reduce.4
where the time goes:
time: 1840 us; the launch traced here: 1830 us
  waiting for transfers between devices  1400 us (76%)
  blocking collectives  236 us (13%)
  local copies, waits for them, and re-layouts  67.1 us (4%)
  starting transfers between devices  43.9 us (2%)
  matrix products  39.6 us (2%)
  other arithmetic  29 us (2%)
    psum x2, waiting for transfers between devices, precondition(): restricted = lax.psum(partial_sum, ('gy', 'gz'))  1390 us
    all_gather x2, blocking collectives, precondition(): coarse = lax.all_gather(owned, ('gy', 'gz'), axis=1, tiled=True)  236 us
  transfers between devices with their start and end apart: 14, of which 4 were waited for; matrix products, arithmetic and copies ran while one was open for 4% of the time, Pallas kernels for 0%

commit v1 on v0

--- a/solution.py
+++ b/solution.py
@@ -5,6 +5,7 @@
 from jax.sharding import PartitionSpec as P
 
 HIGH = lax.Precision.HIGHEST
+_plan_lines = lambda vector, across: jnp.sum(lax.all_gather(vector, across), 0)
 
 
 def with_halo(shard, sides, width):
@@ -94,7 +95,7 @@
     means = jnp.sum(flat, axis=2) * (1.0 / 125.0)
     block = means.reshape(vecs * fields, elements)
     partial_sum = jnp.dot(block, onehot, precision=HIGH)
-    restricted = lax.psum(partial_sum, ("gy", "gz"))
+    restricted = _plan_lines(partial_sum, ("gy", "gz"))
     merged = restricted.reshape(vecs, fields * nagg)
     owned = jnp.einsum("kc,rc->kr", merged, coarse_inverse, precision=HIGH)
     coarse = lax.all_gather(owned, ("gy", "gz"), axis=1, tiled=True)

time: 1840 us -> 624 us (0.34)
  the two profiles are of different devices: /device:TPU:225 before, /device:TPU:33 now
where the time goes in v1:
time: 624 us; the launch traced here: 615 us
  blocking collectives  222 us (36%)
  waiting for transfers between devices  198 us (32%)
  local copies, waits for them, and re-layouts  74.9 us (12%)
  matrix products  41.1 us (7%)
  other arithmetic  36.2 us (6%)
  starting transfers between devices  28 us (4%)
  between operations  14.5 us (2%)
    all_gather x2, blocking collectives, precondition(): coarse = lax.all_gather(owned, ('gy', 'gz'), axis=1, tiled=True)  222 us
    all_gather x2, waiting for transfers between devices, lax.all_gather(vector, across)  170 us
    ppermute x6, waiting for transfers between devices, with_halo(): after = lax.ppermute(initial, axis, down)  21.8 us
    concatenate x2, local copies, waits for them, and re-layouts, operate(): stacked = jnp.concatenate(terms, axis=2)  18.4 us
    ppermute x6, starting transfers between devices, with_halo(): before = lax.ppermute(last, axis, up)  14.9 us
    mul x8, local copies, waits for them, and re-layouts, kron_three(): return jnp.kron(jnp.kron(first, second), third)  13.4 us
    ppermute x6, starting transfers between devices, with_halo(): after = lax.ppermute(initial, axis, down)  13.1 us
  transfers between devices with their start and end apart: 14, of which 5 were waited for; matrix products, arithmetic and copies ran while one was open for 12% of the time, Pallas kernels for 0%

profile of v1, /device:TPU:33, one launch (start us, length us, event | category | flops | bytes accessed | tf_op | source)
XLA Modules:
  0.0 615.0 jit_solution(12993849464196796539)
XLA Ops:
  18.8 3.4 mul.353
  22.2 3.4 mul.364
  27.5 3.4 mul.374
  35.1 80.0 %all-gather.9.cloned.1.call-done = f32[64,20,1024]{2,1,0:T(8,128)} async-done(((f32[1,20,1024]{2,1,0:T(8,128)}), f32[64,20,1024]{2,1,0:T(8,128)}) %all-gather.9.cloned.1.call-update) | async-done | bytes 5242896 | tf_op jit(solution)/shard_map/all_gather | solution.py:8
  115.1 3.2 reduce_sum.37
  119.8 111.1 %all-gather.3 = f32[64,80,4]{1,2,0:T(4,128)S(1)} all-gather(f32[1,80,4]{1,2,0:T(4,128)S(1)} %convolution_bitcast_fusion.7), channel_id=1, replica_groups=mesh['gx'=4,'gy'=8,'gz'=8] {'gy','gz'}, dimensions={0}, use_global_device_ids=true | all-gather | bytes 83200 | tf_op jit(solution)/shard_map/all_gather | solution.py:101
  255.7 3.5 collective-permute-start
  259.2 4.6 fusion.9
  274.3 6.3 %collective-permute-done = f32[2,4,5,25,1,1,128]{6,1,5,4,3,2,0:T(4,128)} collective-permute-done((f32[2,4,5,25,1,1,128]{6,1,5,4,3,2,0:T(4,128)}, f32[2,4,5,25,1,1,128]{6,1,5,4,3,2,0:T(4,128)}, u32[]{:S(2)}, u32[]{:S(2)}) %collective-permute-start) | collective-permute-done | bytes 512032 | tf_op jit(solution)/shard_map/ppermute | solution.py:18
  282.2 7.4 %collective-permute-done.1 = f32[2,4,5,25,1,1,128]{6,1,5,4,3,2,0:T(4,128)} collective-permute-done((f32[2,4,5,25,1,1,128]{6,1,5,4,3,2,0:T(4,128)}, f32[2,4,5,25,1,1,128]{6,1,5,4,3,2,0:T(4,128)}, u32[]{:S(2)}, u32[]{:S(2)}) %collective-permute-start.1) | collective-permute-done | bytes 512032 | tf_op jit(solution)/shard_map/ppermute | solution.py:19
  293.4 9.2 %concatenate.27 = f32[4,5,150,128]{3,2,1,0:T(8,128)S(1)} concatenate(f32[4,5,25,128]{3,2,1,0:T(8,128)} %fusion.63, f32[4,5,25,128]{3,2,1,0:T(8,128)} %get-tuple-element.35, f32[4,5,25,128]{3,2,1,0:T(8,128)} %get-tuple-element.36, f32[4,5,25,128]{3,2,1,0:T(8,128)} %get-tuple-element.37, f32[4,5,25,128]{3,2,1,0:T(8,128)} %get-tuple-element.22, f32[4,5,25,128]{3,2,1,0:T(8,128)S(1)} %get-tuple-element.21), dimensions={2} | concatenate | bytes 3072000 | tf_op jit(solution)/shard_map/concatenate | solution.py:86
  305.0 4.3 fusion.74
  310.3 3.8 convolution_bitcast_fusion.2
  316.0 89.7 %all-gather.11.cloned.1.call-done = f32[64,20,1024]{2,1,0:T(8,128)} async-done(((f32[1,20,1024]{2,1,0:T(8,128)}), f32[64,20,1024]{2,1,0:T(8,128)}) %all-gather.11.cloned.1.call-update) | async-done | bytes 5242896 | tf_op jit(solution)/shard_map/all_gather | solution.py:8
  405.7 3.2 reduce_sum.39
  410.4 111.3 %all-gather.5 = f32[64,80,4]{1,2,0:T(4,128)S(1)} all-gather(f32[1,80,4]{1,2,0:T(4,128)S(1)} %convolution_bitcast_fusion.6), channel_id=1, replica_groups=mesh['gx'=4,'gy'=8,'gz'=8] {'gy','gz'}, dimensions={0}, use_global_device_ids=true | all-gather | bytes 83200 | tf_op jit(solution)/shard_map/all_gather | solution.py:101
  522.4 3.5 bitcast_add_fusion.2
  535.1 3.4 collective-permute-start.6
  548.3 6.2 %fusion.12 = f32[4,128,5,125]{1,3,2,0:T(8,128)} fusion(f32[4,5,125,128,1]{3,1,2,0,4:T(8,128)} %bitcast.224, f32[125,125]{1,0:T(8,128)} %mul.374, f32[5,5]{1,0:T(8,128)S(1)} %copy-done.33, f32[125,125]{1,0:T(8,128)} %mul.364, f32[5,5]{1,0:T(8,128)} %get-tuple-element.66, f32[125,125]{1,0:T(8,128)} %mul.353, f32[5,5]{1,0:T(8,128)} %bitcast.228), kind=kOutput, calls=%fused_computation.23 | convolution fusion | flops 2401953024 | bytes 2747800 | tf_op jit(solution)/shard_map/fqgp,kgpe->kfqe/dot_general | solution.py:60
  566.5 14.4 %collective-permute-done.7 = f32[2,4,5,25,1,1,128]{6,1,5,4,3,2,0:T(4,128)} collective-permute-done((f32[2,4,5,25,1,1,128]{6,1,5,4,3,2,0:T(4,128)}, f32[2,4,5,25,1,1,128]{6,1,5,4,3,2,0:T(4,128)}, u32[]{:S(2)}, u32[]{:S(2)}) %collective-permute-start.7) | collective-permute-done | bytes 512032 | tf_op jit(solution)/shard_map/ppermute | solution.py:19
  584.2 9.2 %concatenate.31 = f32[4,5,150,128]{3,2,1,0:T(8,128)S(1)} concatenate(f32[4,5,25,128]{3,2,1,0:T(8,128)} %get-tuple-element.25, f32[4,5,25,128]{3,2,1,0:T(8,128)} %get-tuple-element.26, f32[4,5,25,128]{3,2,1,0:T(8,128)} %get-tuple-element.27, f32[4,5,25,128]{3,2,1,0:T(8,128)} %get-tuple-element.28, f32[4,5,25,128]{3,2,1,0:T(8,128)} %get-tuple-element.16, ...), dimensions={2} | concatenate | bytes 3072000 | tf_op jit(solution)/shard_map/concatenate | solution.py:86
  593.4 6.2 %fusion.77 = f32[4,5,128,125]{3,2,1,0:T(8,128)} fusion(f32[4,5,150,128]{3,2,1,0:T(8,128)S(1)} %concatenate.31, f32[150,125,1,1]{1,0,3,2:T(8,128)} %constant.10), kind=kOutput, calls=%fused_computation.153 | convolution fusion | flops 576000000 | bytes 2891000 | tf_op jit(solution)/shard_map/sq,kfse->kfqe/dot_general | solution.py:87
  599.6 2.9 copy.88
  602.5 3.1 fusion
  (185 shorter events, 103.7 us)
Async XLA Ops:
  6.5 111.9 %copy-start = (f32[80,5120]{1,0:T(8,128)S(1)}, f32[80,5120]{1,0:T(8,128)}, u32[]{:S(2)}) copy-start(f32[80,5120]{1,0:T(8,128)} %param.16) | copy-start | bytes 4915204
  6.5 108.6 %all-gather.9.cloned.1.call-start = ((), (), s32[]{:S(2)}) async-start(), calls=%async_computation | async-start | bytes 6389760 | tf_op jit(solution)/shard_map/all_gather | solution.py:8
  10.4 395.4 %all-gather.11.cloned.1.call-start = ((), (), s32[]{:S(2)}) async-start(), calls=%async_computation.1 | async-start | bytes 6389760 | tf_op jit(solution)/shard_map/all_gather | solution.py:8
  15.9 16.7 %copy-start.21 = (f32[125,125,1,1]{1,0,2,3:T(8,128)}, f32[125,125,1,1]{1,0,2,3:T(8,128)S(1)}, u32[]{:S(2)}) copy-start(f32[125,125,1,1]{1,0,2,3:T(8,128)S(1)} %reshape.393) | copy-start | bytes 187504
  118.4 112.8 %copy-start.37 = (s32[1,1,128]{2,1,0:T(1,128)S(1)}, s32[1,1,128]{2,1,0:T(1,128)}, u32[]{:S(2)}) copy-start(s32[1,1,128]{2,1,0:T(1,128)} %param.15) | copy-start | bytes 1540
  118.4 113.2 %copy-start.28 = (f32[5,5]{1,0:T(8,128)S(1)}, f32[5,5]{1,0:T(8,128)}, u32[]{:S(2)}) copy-start(f32[5,5]{1,0:T(8,128)} %param.14) | copy-start | bytes 304
  239.3 32.7 %collective-permute-start.2 = (f32[2,4,5,25,1,1,128]{6,1,5,4,3,2,0:T(4,128)}, f32[2,4,5,25,1,1,128]{6,1,5,4,3,2,0:T(4,128)}, u32[]{:S(2)}, u32[]{:S(2)}) collective-permute-start(f32[2,4,5,25,1,1,128]{6,1,5,4,3,2,0:T(4,128)} %copy.60), channel_id=1, source_target_pairs={{0,8},{8,16},{16,24},{24,32},{32,40},{40,48},{48,56},{1,9},{9,17},... | collective-permute-start | bytes 1536008 | tf_op jit(solution)/shard_map/ppermute | solution.py:18
  241.4 31.8 %collective-permute-start.3 = (f32[2,4,5,25,1,1,128]{6,1,5,4,3,2,0:T(4,128)}, f32[2,4,5,25,1,1,128]{6,1,5,4,3,2,0:T(4,128)}, u32[]{:S(2)}, u32[]{:S(2)}) collective-permute-start(f32[2,4,5,25,1,1,128]{6,1,5,4,3,2,0:T(4,128)} %copy.60), channel_id=1, source_target_pairs={{8,0},{16,8},{24,16},{32,24},{40,32},{48,40},{56,48},{9,1},{17,9},... | collective-permute-start | bytes 1536008 | tf_op jit(solution)/shard_map/ppermute | solution.py:19
  246.0 17.9 %collective-permute-start.4 = (f32[2,4,5,25,1,1,1]{3,1,6,5,4,2,0:T(4,128)}, f32[2,4,5,25,1,1,1]{3,1,6,5,4,2,0:T(4,128)S(1)}, u32[]{:S(2)}, u32[]{:S(2)}) collective-permute-start(f32[2,4,5,25,1,1,1]{3,1,6,5,4,2,0:T(4,128)} %copy.64), channel_id=1, source_target_pairs={{0,1},{1,2},{2,3},{3,4},{4,5},{5,6},{6,7},{8,9},{9,10},{10,11},{11... | collective-permute-start | bytes 12008 | tf_op jit(solution)/shard_map/ppermute | solution.py:18
  249.9 9.3 %copy-start.32 = (f32[5,5]{1,0:T(8,128)S(1)}, f32[5,5]{1,0:T(8,128)}, u32[]{:S(2)}) copy-start(f32[5,5]{1,0:T(8,128)} %get-tuple-element.65) | copy-start | bytes 304
  249.9 17.9 %collective-permute-start.5 = (f32[2,4,5,25,1,1,1]{3,1,6,5,4,2,0:T(4,128)}, f32[2,4,5,25,1,1,1]{3,1,6,5,4,2,0:T(4,128)}, u32[]{:S(2)}, u32[]{:S(2)}) collective-permute-start(f32[2,4,5,25,1,1,1]{3,1,6,5,4,2,0:T(4,128)} %copy.65), channel_id=1, source_target_pairs={{1,0},{2,1},{3,2},{4,3},{5,4},{6,5},{7,6},{9,8},{10,9},{11,10},{12... | collective-permute-start | bytes 12008 | tf_op jit(solution)/shard_map/ppermute | solution.py:19
  255.7 25.0 %collective-permute-start = (f32[2,4,5,25,1,1,128]{6,1,5,4,3,2,0:T(4,128)}, f32[2,4,5,25,1,1,128]{6,1,5,4,3,2,0:T(4,128)}, u32[]{:S(2)}, u32[]{:S(2)}) collective-permute-start(f32[2,4,5,25,1,1,128]{6,1,5,4,3,2,0:T(4,128)} %copy.54), channel_id=1, source_target_pairs={{0,64},{64,128},{128,192},{1,65},{65,129},{129,193},{2,66},{66,130... | collective-permute-start | bytes 1536008 | tf_op jit(solution)/shard_map/ppermute | solution.py:18
  263.8 25.8 %collective-permute-start.1 = (f32[2,4,5,25,1,1,128]{6,1,5,4,3,2,0:T(4,128)}, f32[2,4,5,25,1,1,128]{6,1,5,4,3,2,0:T(4,128)}, u32[]{:S(2)}, u32[]{:S(2)}) collective-permute-start(f32[2,4,5,25,1,1,128]{6,1,5,4,3,2,0:T(4,128)} %copy.54), channel_id=1, source_target_pairs={{64,0},{128,64},{192,128},{65,1},{129,65},{193,129},{66,2},{130,66... | collective-permute-start | bytes 1536008 | tf_op jit(solution)/shard_map/ppermute | solution.py:19
  272.0 9.8 %copy-start.12 = (f32[1,4,5,25,1,1,128]{6,3,2,1,5,4,0:T(8,128)S(1)}, f32[1,4,5,25,1,1,128]{6,3,2,1,5,4,0:T(8,128)}, u32[]{:S(2)}) copy-start(f32[1,4,5,25,1,1,128]{6,3,2,1,5,4,0:T(8,128)} %copy-done.11) | copy-start | bytes 768004
  529.1 9.5 %copy-start.13 = (f32[1,4,5,25,1,1,128]{6,3,2,1,5,4,0:T(8,128)}, f32[1,4,5,25,1,1,128]{6,3,2,1,5,4,0:T(8,128)S(1)}, u32[]{:S(2)}) copy-start(f32[1,4,5,25,1,1,128]{6,3,2,1,5,4,0:T(8,128)S(1)} %get-tuple-element.29) | copy-start | bytes 768004
  529.1 9.5 %copy-start.14 = (f32[1,4,5,25,1,1,128]{6,3,2,1,5,4,0:T(8,128)}, f32[1,4,5,25,1,1,128]{6,3,2,1,5,4,0:T(8,128)S(1)}, u32[]{:S(2)}) copy-start(f32[1,4,5,25,1,1,128]{6,3,2,1,5,4,0:T(8,128)S(1)} %get-tuple-element.32) | copy-start | bytes 768004
  530.5 32.0 %collective-permute-start.8 = (f32[2,4,5,25,1,1,128]{6,1,5,4,3,2,0:T(4,128)}, f32[2,4,5,25,1,1,128]{6,1,5,4,3,2,0:T(4,128)}, u32[]{:S(2)}, u32[]{:S(2)}) collective-permute-start(f32[2,4,5,25,1,1,128]{6,1,5,4,3,2,0:T(4,128)} %copy.80), channel_id=1, source_target_pairs={{0,8},{8,16},{16,24},{24,32},{32,40},{40,48},{48,56},{1,9},{9,17},... | collective-permute-start | bytes 1536008 | tf_op jit(solution)/shard_map/ppermute | solution.py:18
  532.6 31.1 %collective-permute-start.9 = (f32[2,4,5,25,1,1,128]{6,1,5,4,3,2,0:T(4,128)}, f32[2,4,5,25,1,1,128]{6,1,5,4,3,2,0:T(4,128)}, u32[]{:S(2)}, u32[]{:S(2)}) collective-permute-start(f32[2,4,5,25,1,1,128]{6,1,5,4,3,2,0:T(4,128)} %copy.80), channel_id=1, source_target_pairs={{8,0},{16,8},{24,16},{32,24},{40,32},{48,40},{56,48},{9,1},{17,9},... | collective-permute-start | bytes 1536008 | tf_op jit(solution)/shard_map/ppermute | solution.py:19
  535.1 29.8 %collective-permute-start.6 = (f32[2,4,5,25,1,1,128]{6,1,5,4,3,2,0:T(4,128)}, f32[2,4,5,25,1,1,128]{6,1,5,4,3,2,0:T(4,128)}, u32[]{:S(2)}, u32[]{:S(2)}) collective-permute-start(f32[2,4,5,25,1,1,128]{6,1,5,4,3,2,0:T(4,128)} %copy.75), channel_id=1, source_target_pairs={{0,64},{64,128},{128,192},{1,65},{65,129},{129,193},{2,66},{66,130... | collective-permute-start | bytes 1536008 | tf_op jit(solution)/shard_map/ppermute | solution.py:18
  538.6 9.6 %copy-start.33 = (f32[5,5]{1,0:T(8,128)S(1)}, f32[5,5]{1,0:T(8,128)}, u32[]{:S(2)}) copy-start(f32[5,5]{1,0:T(8,128)} %get-tuple-element.65) | copy-start | bytes 304
  541.9 12.5 %collective-permute-start.10 = (f32[2,4,5,25,1,1,1]{3,1,6,5,4,2,0:T(4,128)}, f32[2,4,5,25,1,1,1]{3,1,6,5,4,2,0:T(4,128)S(1)}, u32[]{:S(2)}, u32[]{:S(2)}) collective-permute-start(f32[2,4,5,25,1,1,1]{3,1,6,5,4,2,0:T(4,128)} %copy.84), channel_id=1, source_target_pairs={{0,1},{1,2},{2,3},{3,4},{4,5},{5,6},{6,7},{8,9},{9,10},{10,11},{11... | collective-permute-start | bytes 12008 | tf_op jit(solution)/shard_map/ppermute | solution.py:18
  545.9 12.6 %collective-permute-start.11 = (f32[2,4,5,25,1,1,1]{3,1,6,5,4,2,0:T(4,128)}, f32[2,4,5,25,1,1,1]{3,1,6,5,4,2,0:T(4,128)}, u32[]{:S(2)}, u32[]{:S(2)}) collective-permute-start(f32[2,4,5,25,1,1,1]{3,1,6,5,4,2,0:T(4,128)} %copy.85), channel_id=1, source_target_pairs={{1,0},{2,1},{3,2},{4,3},{5,4},{6,5},{7,6},{9,8},{10,9},{11,10},{12... | collective-permute-start | bytes 12008 | tf_op jit(solution)/shard_map/ppermute | solution.py:19
  554.4 26.4 %collective-permute-start.7 = (f32[2,4,5,25,1,1,128]{6,1,5,4,3,2,0:T(4,128)}, f32[2,4,5,25,1,1,128]{6,1,5,4,3,2,0:T(4,128)}, u32[]{:S(2)}, u32[]{:S(2)}) collective-permute-start(f32[2,4,5,25,1,1,128]{6,1,5,4,3,2,0:T(4,128)} %copy.75), channel_id=1, source_target_pairs={{64,0},{128,64},{192,128},{65,1},{129,65},{193,129},{66,2},{130,66... | collective-permute-start | bytes 1536008 | tf_op jit(solution)/shard_map/ppermute | solution.py:19
  566.3 15.7 %copy-start.6 = (f32[1,4,5,25,1,1,128]{6,3,2,1,4,5,0:T(8,128)S(1)}, f32[1,4,5,25,1,1,128]{6,3,2,1,4,5,0:T(8,128)}, u32[]{:S(2)}) copy-start(f32[1,4,5,25,1,1,128]{6,3,2,1,4,5,0:T(8,128)} %copy-done.5) | copy-start | bytes 768004
  (29 other events, 151.9 us)
Sparse Core Ops, SparseCore 0:
  11.1 104.0 all-gather.8
  310.4 95.2 all-gather.10
